TPU v7x, 256 devices: a whole 4x4x8 slice. The times are simulated.
256 devices in a mesh: gx: 32 (over x, y, core), gy: 8 (over z).
Axes of the slice: x: 4, y: 4, z: 8, core: 2. Of those that a mesh axis runs over, the one named last changes fastest.
Arguments:
- orbitals: float32 [64, 128, 64, 128], P(None, 'gx', 'gy'), may hold values from -60 to 60, as said below
- potential: float32 [128, 64, 128], P('gx', 'gy'), may hold values from 0.2 to 2
Outputs:
- basis: float32 [64, 128, 64, 128], P(None, 'gx', 'gy')
- factor: float32 [64, 64], replicated
Inputs may be any that keep to these rules, and one draw needn't show every extreme that they name: `orbitals`: Real-valued entries.
All inputs are finite; a program needn't handle non-finite values.
Results may differ from a plain program's by a relative error of at most 0.00011.
Values sent between devices are 32-bit elements; how exact they have to be, the bound alone decides.
No kernel may reach another device: no remote copies, remote signals or barrier semaphores. Data moves between devices by JAX's collectives and lax.ppermute only.
A program may use at most 64 MiB of HBM per device.

v0:
```python
import jax
import jax.numpy as jnp
from jax import lax
from jax.sharding import PartitionSpec as P


def extended(cells, sides, width):
    for axis, dim in sides:
        count = lax.axis_size(axis)
        head = lax.slice_in_dim(cells, 0, width, axis=dim)
        tail = lax.slice_in_dim(cells, cells.shape[dim] - width, cells.shape[dim], axis=dim)
        cells = jnp.concatenate(
            [
                lax.ppermute(tail, axis, [(i, (i + 1) % count) for i in range(count)]),
                cells,
                lax.ppermute(head, axis, [((i + 1) % count, i) for i in range(count)]),
            ],
            axis=dim,
        )
    return cells


def apply_ham(padded, pot):
    core = padded[:, 2:-2, 2:-2]
    total = -7.5 * core
    total = total + 4.0 / 3.0 * (padded[:, 3:-1, 2:-2] + padded[:, 1:-3, 2:-2])
    total = total - 1.0 / 12.0 * (padded[:, 4:, 2:-2] + padded[:, :-4, 2:-2])
    total = total + 4.0 / 3.0 * (padded[:, 2:-2, 3:-1] + padded[:, 2:-2, 1:-3])
    total = total - 1.0 / 12.0 * (padded[:, 2:-2, 4:] + padded[:, 2:-2, :-4])
    total = total + 4.0 / 3.0 * (jnp.roll(core, 1, 3) + jnp.roll(core, -1, 3))
    total = total - 1.0 / 12.0 * (jnp.roll(core, 2, 3) + jnp.roll(core, -2, 3))
    return -0.5 * total + pot[None] * core


def with_faces(field):
    return extended(field, (("gx", 1), ("gy", 2)), 2)


def upper_factor(gram):
    order = gram.shape[0]
    index = jnp.arange(order)

    def column_step(col, lower):
        row_now = lax.dynamic_slice_in_dim(lower, col, 1, 0)[0]
        target = lax.dynamic_slice_in_dim(gram, col, 1, 1)[:, 0]
        column = target - jnp.dot(
            lower, row_now, precision=lax.Precision.HIGHEST, preferred_element_type=jnp.float32
        )
        pivot = jnp.sqrt(jnp.sum(jnp.where(index == col, column, 0.0)))
        values = jnp.where(index == col, pivot, column / pivot)
        values = jnp.where(index >= col, values, 0.0)
        return jnp.where(index[None, :] == col, values[:, None], lower)

    lower = lax.fori_loop(0, order, column_step, jnp.zeros_like(gram))
    return lower.T


def upper_inverse(upper):
    order = upper.shape[0]
    index = jnp.arange(order)

    def row_step(step, inverse):
        row = order - 1 - step
        upper_row = lax.dynamic_slice_in_dim(upper, row, 1, 0)[0]
        pivot = jnp.sum(jnp.where(index == row, upper_row, 0.0))
        rest = jnp.dot(
            upper_row, inverse, precision=lax.Precision.HIGHEST, preferred_element_type=jnp.float32
        )
        unit = jnp.where(index == row, 1.0, 0.0).astype(jnp.float32)
        new_row = (unit - rest) / pivot
        return jnp.where(index[:, None] == row, new_row[None, :], inverse)

    return lax.fori_loop(0, order, row_step, jnp.zeros_like(upper))


def shards(orbitals, potential):
    first = (apply_ham(with_faces(orbitals), potential) - 5.5 * orbitals) / 4.5
    applied = apply_ham(with_faces(first), potential)
    filtered = 2.0 * (applied - 5.5 * first) / 4.5 - orbitals
    width = filtered.shape[0]
    flat = filtered.reshape(width, -1)
    cells = flat.shape[1] * lax.axis_size("gx") * lax.axis_size("gy")
    local_gram = (
        jnp.dot(flat, flat.T, precision=lax.Precision.HIGHEST, preferred_element_type=jnp.float32)
        / cells
    )
    factor = upper_factor(lax.psum(local_gram, ("gx", "gy")))
    inverse = upper_inverse(factor)
    solved = jnp.dot(
        inverse.T, flat, precision=lax.Precision.HIGHEST, preferred_element_type=jnp.float32
    )
    basis = (solved * jnp.sqrt(jnp.float32(cells))).reshape(filtered.shape)
    return (basis, factor)


def solution(mesh):
    return jax.shard_map(
        shards,
        mesh=mesh,
        in_specs=(P(None, "gx", "gy", None), P("gx", "gy", None)),
        out_specs=(P(None, "gx", "gy", None), P()),
        check_vma=False,
    )
```

profile of v0, /device:TPU:1, one launch (start us, length us, event | category | flops | bytes accessed | tf_op | source)
XLA Modules:
  0.0 353.4 jit_solution(158170441676691293)
XLA Ops:
  0.6 2.4 fusion.60
  3.0 3.2 collective-permute-start
  8.3 4.5 %collective-permute-done = f32[64,2,8,128]{3,2,1,0:T(8,128)S(1)} collective-permute-done((f32[64,2,8,128]{3,2,1,0:T(8,128)}, f32[64,2,8,128]{3,2,1,0:T(8,128)S(1)}, u32[]{:S(2)}, u32[]{:S(2)}) %collective-permute-start) | collective-permute-done | bytes 524320 | tf_op jit(solution)/shard_map/ppermute | solution.py:16
  13.7 5.7 %collective-permute-start.2 = (f32[64,8,2,128]{3,1,2,0:T(8,128)S(1)}, f32[64,8,2,128]{3,1,2,0:T(8,128)S(1)}, u32[]{:S(2)}, u32[]{:S(2)}) collective-permute-start(f32[64,8,2,128]{3,1,2,0:T(8,128)S(1)} %get-tuple-element.266), channel_id=1, source_target_pairs={{1,0},{2,1},{3,2},{4,3},{5,4},{6,5},{7,6},{0,7},{9,8},{10,9},{11,1... | collective-permute-start | bytes 1572872 | tf_op jit(solution)/shard_map/ppermute | solution.py:16
  20.6 4.8 %collective-permute-done.2 = f32[64,8,2,128]{3,1,2,0:T(8,128)S(1)} collective-permute-done((f32[64,8,2,128]{3,1,2,0:T(8,128)S(1)}, f32[64,8,2,128]{3,1,2,0:T(8,128)S(1)}, u32[]{:S(2)}, u32[]{:S(2)}) %collective-permute-start.2) | collective-permute-done | bytes 524320 | tf_op jit(solution)/shard_map/ppermute | solution.py:16
  25.4 3.1 collective-permute-done.3
  28.6 7.3 %broadcast_multiply_fusion = (f32[64,4,8,128]{3,1,2,0:T(4,128)S(1)}, f32[64,4,8,128]{3,1,2,0:T(4,128)S(1)}) fusion(f32[64,4,8,128]{3,1,2,0:T(4,128)S(1)} %copy.55, f32[4,8,128]{2,0,1:T(4,128)S(1)} %copy.71, f32[64,4,8,2]{3,1,2,0:T(4,128)S(1)} %get-tuple-element.285, f32[64,4,8,126]{3,1,2,0:T(4,128)S(1)} %get-tuple-element.287, ...), kind=kLoop, calls=%fused_computation.105 | loop fusion | flops 11796480 | bytes 9453568 | tf_op jit(solution)/shard_map/div | solution.py:77
  36.4 9.8 %collective-permute-start.4 = (f32[64,2,8,128]{3,2,1,0:T(8,128)S(1)}, f32[64,2,8,128]{3,2,1,0:T(8,128)S(1)}, u32[]{:S(2)}, u32[]{:S(2)}) collective-permute-start(f32[64,2,8,128]{3,2,1,0:T(8,128)S(1)} %copy.74), channel_id=1, source_target_pairs={{8,0},{16,8},{24,16},{32,24},{40,32},{48,40},{56,48},{64,56},{72,6... | collective-permute-start | bytes 1572872 | tf_op jit(solution)/shard_map/ppermute | solution.py:16
  47.7 3.3 collective-permute-done.4
  51.3 1.3 collective-permute-done.5
  53.3 1.5 collective-permute-start.7
  56.0 5.3 %collective-permute-done.6 = f32[64,8,2,128]{3,1,2,0:T(8,128)S(1)} collective-permute-done((f32[64,8,2,128]{3,1,2,0:T(8,128)S(1)}, f32[64,8,2,128]{3,1,2,0:T(8,128)S(1)}, u32[]{:S(2)}, u32[]{:S(2)}) %collective-permute-start.6) | collective-permute-done | bytes 524320 | tf_op jit(solution)/shard_map/ppermute | solution.py:16
  61.3 1.3 collective-permute-done.7
  62.6 7.5 %multiply_subtract_fusion = f32[64,4,8,128]{3,1,2,0:T(4,128)S(1)} fusion(f32[64,4,8,128]{3,1,2,0:T(4,128)S(1)} %get-tuple-element.261, f32[64,4,8,2]{3,1,2,0:T(4,128)S(1)} %get-tuple-element.275, f32[64,4,8,126]{3,1,2,0:T(4,128)S(1)} %get-tuple-element.277, f32[64,4,8,126]{3,1,2,0:T(4,128)S(1)} %get-tuple-element.276, ...), kind=kLoop, calls=%fused_computation.97 | loop fusion | flops 12058624 | bytes 10502144 | tf_op jit(solution)/shard_map/sub | solution.py:79
  70.1 2.1 fusion.17
  72.2 81.9 %psum.7 = f32[64,64]{1,0:T(8,128)S(1)} all-reduce(f32[64,64]{1,0:T(8,128)S(1)} %fusion.17), channel_id=1, replica_groups=mesh['gx'=32,'gy'=8] {'gx','gy'}, use_global_device_ids=true, to_apply=%region_0.1 | all-reduce | flops 4096 | bytes 32768 | tf_op jit(solution)/shard_map/psum | solution.py:87
  154.2 101.3 %while.32 = (s32[]{:T(128)}, f32[64,64]{1,0:T(8,128)S(1)}, f32[64,64]{0,1:T(8,128)S(1)}, s32[]{:T(128)}, s32[]{:T(128)}) while((s32[]{:T(128)}, f32[64,64]{1,0:T(8,128)S(1)}, f32[64,64]{0,1:T(8,128)S(1)}, s32[]{:T(128)}, s32[]{:T(128)}) %tuple.94), condition=%wide.region_3.4_spmd.clone.clone, body=%wide.region_1.3_spmd.clone.clone.sunk | while | flops 62082 | bytes 102112 | solution.py:54
  255.6 95.1 %while.31 = (s32[]{:T(128)}, f32[64,64]{1,0:T(8,128)S(1)}, f32[64,64]{1,0:T(8,128)S(1)}, s32[]{:T(128)}, s32[]{:T(128)}, /*index=5*/s32[]{:T(128)}, s32[]{:T(128)}) while((s32[]{:T(128)}, f32[64,64]{1,0:T(8,128)S(1)}, f32[64,64]{1,0:T(8,128)S(1)}, s32[]{:T(128)}, s32[]{:T(128)}, /*index=5*/s32[]{:T(128)}, s32[]{:T(128)}) %tuple.100), condition=%wide.region_6.7_spmd.clone, body=%wide.region_4.6_spmd.clone.sunk | while | flops 61958 | bytes 67106 | solution.py:73
  256.2 0.8 fusion.75
  257.7 0.8 fusion.75
  259.1 0.8 fusion.75
  262.1 0.8 fusion.75
  350.6 1.6 fusion.16
  352.2 1.2 copy.89
  (609 shorter events, 155.8 us)
Async XLA Ops:
  0.6 5.6 %copy-start = (f32[64,4,8,128]{3,2,1,0:T(8,128)S(1)}, f32[64,4,8,128]{3,2,1,0:T(8,128)}, u32[]{:S(2)}) copy-start(f32[64,4,8,128]{3,2,1,0:T(8,128)} %param.6) | copy-start | bytes 3145732
  3.0 9.8 %collective-permute-start = (f32[64,2,8,128]{3,2,1,0:T(8,128)}, f32[64,2,8,128]{3,2,1,0:T(8,128)S(1)}, u32[]{:S(2)}, u32[]{:S(2)}) collective-permute-start(f32[64,2,8,128]{3,2,1,0:T(8,128)} %get-tuple-element.279), channel_id=1, source_target_pairs={{8,0},{16,8},{24,16},{32,24},{40,32},{48,40},{56,48},{64,56},{72,6... | collective-permute-start | bytes 1572872 | tf_op jit(solution)/shard_map/ppermute | solution.py:16
  6.2 0.7 copy-start.1
  6.2 6.8 %collective-permute-start.1 = (f32[64,2,8,128]{3,2,1,0:T(8,128)}, f32[64,2,8,128]{3,2,1,0:T(8,128)S(1)}, u32[]{:S(2)}, u32[]{:S(2)}) collective-permute-start(f32[64,2,8,128]{3,2,1,0:T(8,128)} %get-tuple-element.278), channel_id=1, source_target_pairs={{0,8},{8,16},{16,24},{24,32},{32,40},{40,48},{48,56},{56,64},{64,7... | collective-permute-start | bytes 1572872 | tf_op jit(solution)/shard_map/ppermute | solution.py:14
  13.7 11.8 %collective-permute-start.2 = (f32[64,8,2,128]{3,1,2,0:T(8,128)S(1)}, f32[64,8,2,128]{3,1,2,0:T(8,128)S(1)}, u32[]{:S(2)}, u32[]{:S(2)}) collective-permute-start(f32[64,8,2,128]{3,1,2,0:T(8,128)S(1)} %get-tuple-element.266), channel_id=1, source_target_pairs={{1,0},{2,1},{3,2},{4,3},{5,4},{6,5},{7,6},{0,7},{9,8},{10,9},{11,1... | collective-permute-start | bytes 1572872 | tf_op jit(solution)/shard_map/ppermute | solution.py:16
  19.3 9.2 %collective-permute-start.3 = (f32[64,8,2,128]{3,1,2,0:T(8,128)S(1)}, f32[64,8,2,128]{3,1,2,0:T(8,128)S(1)}, u32[]{:S(2)}, u32[]{:S(2)}) collective-permute-start(f32[64,8,2,128]{3,1,2,0:T(8,128)S(1)} %get-tuple-element.267), channel_id=1, source_target_pairs={{0,1},{1,2},{2,3},{3,4},{4,5},{5,6},{6,7},{7,0},{8,9},{9,10},{10,1... | collective-permute-start | bytes 1572872 | tf_op jit(solution)/shard_map/ppermute | solution.py:14
  36.4 14.6 %collective-permute-start.4 = (f32[64,2,8,128]{3,2,1,0:T(8,128)S(1)}, f32[64,2,8,128]{3,2,1,0:T(8,128)S(1)}, u32[]{:S(2)}, u32[]{:S(2)}) collective-permute-start(f32[64,2,8,128]{3,2,1,0:T(8,128)S(1)} %copy.74), channel_id=1, source_target_pairs={{8,0},{16,8},{24,16},{32,24},{40,32},{48,40},{56,48},{64,56},{72,6... | collective-permute-start | bytes 1572872 | tf_op jit(solution)/shard_map/ppermute | solution.py:16
  46.2 6.4 %collective-permute-start.5 = (f32[64,2,8,128]{3,2,1,0:T(8,128)S(1)}, f32[64,2,8,128]{3,2,1,0:T(8,128)S(1)}, u32[]{:S(2)}, u32[]{:S(2)}) collective-permute-start(f32[64,2,8,128]{3,2,1,0:T(8,128)S(1)} %copy.76), channel_id=1, source_target_pairs={{0,8},{8,16},{16,24},{24,32},{32,40},{40,48},{48,56},{56,64},{64,7... | collective-permute-start | bytes 1572872 | tf_op jit(solution)/shard_map/ppermute | solution.py:14
  53.2 8.1 %collective-permute-start.6 = (f32[64,8,2,128]{3,1,2,0:T(8,128)S(1)}, f32[64,8,2,128]{3,1,2,0:T(8,128)S(1)}, u32[]{:S(2)}, u32[]{:S(2)}) collective-permute-start(f32[64,8,2,128]{3,1,2,0:T(8,128)S(1)} %get-tuple-element.264), channel_id=1, source_target_pairs={{1,0},{2,1},{3,2},{4,3},{5,4},{6,5},{7,6},{0,7},{9,8},{10,9},{11,1... | collective-permute-start | bytes 1572872 | tf_op jit(solution)/shard_map/ppermute | solution.py:16
  53.3 9.3 %collective-permute-start.7 = (f32[64,8,2,128]{3,1,2,0:T(8,128)S(1)}, f32[64,8,2,128]{3,1,2,0:T(8,128)S(1)}, u32[]{:S(2)}, u32[]{:S(2)}) collective-permute-start(f32[64,8,2,128]{3,1,2,0:T(8,128)S(1)} %get-tuple-element.265), channel_id=1, source_target_pairs={{0,1},{1,2},{2,3},{3,4},{4,5},{5,6},{6,7},{7,0},{8,9},{9,10},{10,1... | collective-permute-start | bytes 1572872 | tf_op jit(solution)/shard_map/ppermute | solution.py:14
  350.6 1.6 copy-start.2
where the time goes:
time: 355 us; the launch traced here: 353 us
  matrix products  103 us (29%)
  blocking collectives  81.9 us (23%)
  other arithmetic  66.1 us (19%)
  loops' own time  46 us (13%)
  waiting for transfers between devices  23.6 us (7%)
  starting transfers between devices  20.4 us (6%)
  local copies, waits for them, and re-layouts  11.1 us (3%)
    psum x1, blocking collectives, shards(): factor = upper_factor(lax.psum(local_gram, ('gx', 'gy')))  81.9 us
    dot_general x64, matrix products, row_step(): jnp.dot(upper_row, inverse, precision=lax.Precision.HIGHEST, preferred_el...  50.1 us
    dot_general x64, matrix products, column_step(): jnp.dot(lower, row_now, precision=lax.Precision.HIGHEST, preferred_elemen...  49.5 us
    another operation x1, loops' own time, upper_factor(): lower = lax.fori_loop(0, order, column_step, jnp.zeros_like(gram))  45.6 us
    reduce_sum x64, other arithmetic, row_step(): pivot = jnp.sum(jnp.where(index == row, upper_row, 0.0))  39.3 us
    ppermute x4, starting transfers between devices, extended(): lax.ppermute(head, axis, [((i + 1) % count, i) for i in range(count)])  18.7 us
    ppermute x4, waiting for transfers between devices, extended(): lax.ppermute(head, axis, [((i + 1) % count, i) for i in range(count)])  17.9 us
    sub x1, other arithmetic, shards(): filtered = 2.0 * (applied - 5.5 * first) / 4.5 - orbitals  7.45 us
  transfers between devices with their start and end apart: 8, of which 7 were waited for; matrix products, arithmetic and copies ran while one was open for 2% of the time, Pallas kernels for 0%

commit v1 on v0

--- a/solution.py
+++ b/solution.py
@@ -2,6 +2,8 @@
 import jax.numpy as jnp
 from jax import lax
 from jax.sharding import PartitionSpec as P
+
+hold_windows = lambda sample: lax.psum(lax.psum(sample, "gy"), "gx")
 
 
 def extended(cells, sides, width):
@@ -84,7 +86,7 @@
         jnp.dot(flat, flat.T, precision=lax.Precision.HIGHEST, preferred_element_type=jnp.float32)
         / cells
     )
-    factor = upper_factor(lax.psum(local_gram, ("gx", "gy")))
+    factor = upper_factor(hold_windows(local_gram))
     inverse = upper_inverse(factor)
     solved = jnp.dot(
         inverse.T, flat, precision=lax.Precision.HIGHEST, preferred_element_type=jnp.float32

time: 355 us -> 430 us (1.21)
  blocking collectives: 81.9 us -> 155 us
    psum x1 -> x2, blocking collectives: 81.9 us -> 155 us  [hold_windows = lambda sample: lax.psum(lax.psum(sample, 'gy'), 'gx')]
  transfers between devices with their start and end apart: 8 -> 8, of which waited for: 7 -> 7; matrix products, arithmetic and copies ran while one was open for 2% -> 1% of each run, Pallas kernels for 0% -> 0%
where the time goes in v1:
time: 430 us; the launch traced here: 427 us
  blocking collectives  155 us (36%)
  matrix products  103 us (24%)
  other arithmetic  66.1 us (15%)
  loops' own time  46 us (11%)
  waiting for transfers between devices  23.6 us (5%)
  starting transfers between devices  20.4 us (5%)
  local copies, waits for them, and re-layouts  11.1 us (3%)
    psum x2, blocking collectives, hold_windows = lambda sample: lax.psum(lax.psum(sample, 'gy'), 'gx')  155 us
    dot_general x64, matrix products, row_step(): jnp.dot(upper_row, inverse, precision=lax.Precision.HIGHEST, preferred_el...  50.1 us
    dot_general x64, matrix products, column_step(): jnp.dot(lower, row_now, precision=lax.Precision.HIGHEST, preferred_elemen...  49.5 us
    another operation x1, loops' own time, upper_factor(): lower = lax.fori_loop(0, order, column_step, jnp.zeros_like(gram))  45.6 us
    reduce_sum x64, other arithmetic, row_step(): pivot = jnp.sum(jnp.where(index == row, upper_row, 0.0))  39.3 us
    ppermute x4, starting transfers between devices, extended(): lax.ppermute(head, axis, [((i + 1) % count, i) for i in range(count)])  18.7 us
    ppermute x4, waiting for transfers between devices, extended(): lax.ppermute(head, axis, [((i + 1) % count, i) for i in range(count)])  17.9 us
  transfers between devices with their start and end apart: 8, of which 7 were waited for; matrix products, arithmetic and copies ran while one was open for 1% of the time, Pallas kernels for 0%

profile of v1, /device:TPU:1, one launch (start us, length us, event | category | flops | bytes accessed | tf_op | source)
XLA Modules:
  0.0 426.7 jit_solution(15361000754226975613)
XLA Ops:
  0.6 2.3 fusion.60
  3.0 3.2 collective-permute-start
  8.3 4.5 %collective-permute-done = f32[64,2,8,128]{3,2,1,0:T(8,128)S(1)} collective-permute-done((f32[64,2,8,128]{3,2,1,0:T(8,128)}, f32[64,2,8,128]{3,2,1,0:T(8,128)S(1)}, u32[]{:S(2)}, u32[]{:S(2)}) %collective-permute-start) | collective-permute-done | bytes 524320 | tf_op jit(solution)/shard_map/ppermute | solution.py:18
  13.6 5.7 %collective-permute-start.2 = (f32[64,8,2,128]{3,1,2,0:T(8,128)S(1)}, f32[64,8,2,128]{3,1,2,0:T(8,128)S(1)}, u32[]{:S(2)}, u32[]{:S(2)}) collective-permute-start(f32[64,8,2,128]{3,1,2,0:T(8,128)S(1)} %get-tuple-element.266), channel_id=1, source_target_pairs={{1,0},{2,1},{3,2},{4,3},{5,4},{6,5},{7,6},{0,7},{9,8},{10,9},{11,1... | collective-permute-start | bytes 1572872 | tf_op jit(solution)/shard_map/ppermute | solution.py:18
  20.6 4.8 %collective-permute-done.2 = f32[64,8,2,128]{3,1,2,0:T(8,128)S(1)} collective-permute-done((f32[64,8,2,128]{3,1,2,0:T(8,128)S(1)}, f32[64,8,2,128]{3,1,2,0:T(8,128)S(1)}, u32[]{:S(2)}, u32[]{:S(2)}) %collective-permute-start.2) | collective-permute-done | bytes 524320 | tf_op jit(solution)/shard_map/ppermute | solution.py:18
  25.4 3.1 collective-permute-done.3
  28.5 7.3 %broadcast_multiply_fusion = (f32[64,4,8,128]{3,1,2,0:T(4,128)S(1)}, f32[64,4,8,128]{3,1,2,0:T(4,128)S(1)}) fusion(f32[64,4,8,128]{3,1,2,0:T(4,128)S(1)} %copy.55, f32[4,8,128]{2,0,1:T(4,128)S(1)} %copy.71, f32[64,4,8,2]{3,1,2,0:T(4,128)S(1)} %get-tuple-element.285, f32[64,4,8,126]{3,1,2,0:T(4,128)S(1)} %get-tuple-element.287, ...), kind=kLoop, calls=%fused_computation.105 | loop fusion | flops 11796480 | bytes 9453568 | tf_op jit(solution)/shard_map/div | solution.py:79
  36.4 9.8 %collective-permute-start.4 = (f32[64,2,8,128]{3,2,1,0:T(8,128)S(1)}, f32[64,2,8,128]{3,2,1,0:T(8,128)S(1)}, u32[]{:S(2)}, u32[]{:S(2)}) collective-permute-start(f32[64,2,8,128]{3,2,1,0:T(8,128)S(1)} %copy.74), channel_id=1, source_target_pairs={{8,0},{16,8},{24,16},{32,24},{40,32},{48,40},{56,48},{64,56},{72,6... | collective-permute-start | bytes 1572872 | tf_op jit(solution)/shard_map/ppermute | solution.py:18
  47.7 3.3 collective-permute-done.4
  51.3 1.3 collective-permute-done.5
  53.3 1.5 collective-permute-start.7
  56.0 5.3 %collective-permute-done.6 = f32[64,8,2,128]{3,1,2,0:T(8,128)S(1)} collective-permute-done((f32[64,8,2,128]{3,1,2,0:T(8,128)S(1)}, f32[64,8,2,128]{3,1,2,0:T(8,128)S(1)}, u32[]{:S(2)}, u32[]{:S(2)}) %collective-permute-start.6) | collective-permute-done | bytes 524320 | tf_op jit(solution)/shard_map/ppermute | solution.py:18
  61.3 1.3 collective-permute-done.7
  62.6 7.5 %multiply_subtract_fusion = f32[64,4,8,128]{3,1,2,0:T(4,128)S(1)} fusion(f32[64,4,8,128]{3,1,2,0:T(4,128)S(1)} %get-tuple-element.261, f32[64,4,8,2]{3,1,2,0:T(4,128)S(1)} %get-tuple-element.275, f32[64,4,8,126]{3,1,2,0:T(4,128)S(1)} %get-tuple-element.277, f32[64,4,8,126]{3,1,2,0:T(4,128)S(1)} %get-tuple-element.276, ...), kind=kLoop, calls=%fused_computation.97 | loop fusion | flops 12058624 | bytes 10502144 | tf_op jit(solution)/shard_map/sub | solution.py:81
  70.1 2.1 fusion.17
  72.2 20.1 %psum.14 = f32[64,64]{1,0:T(8,128)S(1)} all-reduce(f32[64,64]{1,0:T(8,128)S(1)} %fusion.17), channel_id=1, replica_groups=mesh['gx'=32,'gy'=8] {'gy'}, use_global_device_ids=true, to_apply=%region_0.1 | all-reduce | flops 4096 | bytes 32768 | tf_op jit(solution)/shard_map/psum | solution.py:6
  92.4 135.0 %psum.15 = f32[64,64]{1,0:T(8,128)S(1)} all-reduce(f32[64,64]{1,0:T(8,128)S(1)} %psum.14), channel_id=1, replica_groups=mesh['gx'=32,'gy'=8] {'gx'}, use_global_device_ids=true, to_apply=%region_1.2 | all-reduce | flops 4096 | bytes 32768 | tf_op jit(solution)/shard_map/psum | solution.py:6
  227.4 101.3 %while.32 = (s32[]{:T(128)}, f32[64,64]{1,0:T(8,128)S(1)}, f32[64,64]{0,1:T(8,128)S(1)}, s32[]{:T(128)}, s32[]{:T(128)}) while((s32[]{:T(128)}, f32[64,64]{1,0:T(8,128)S(1)}, f32[64,64]{0,1:T(8,128)S(1)}, s32[]{:T(128)}, s32[]{:T(128)}) %tuple.94), condition=%wide.region_4.5_spmd.clone.clone, body=%wide.region_2.4_spmd.clone.clone.sunk | while | flops 62082 | bytes 102112 | solution.py:56
  328.8 95.1 %while.31 = (s32[]{:T(128)}, f32[64,64]{1,0:T(8,128)S(1)}, f32[64,64]{1,0:T(8,128)S(1)}, s32[]{:T(128)}, s32[]{:T(128)}, /*index=5*/s32[]{:T(128)}, s32[]{:T(128)}) while((s32[]{:T(128)}, f32[64,64]{1,0:T(8,128)S(1)}, f32[64,64]{1,0:T(8,128)S(1)}, s32[]{:T(128)}, s32[]{:T(128)}, /*index=5*/s32[]{:T(128)}, s32[]{:T(128)}) %tuple.100), condition=%wide.region_7.8_spmd.clone, body=%wide.region_5.7_spmd.clone.sunk | while | flops 61958 | bytes 67106 | solution.py:75
  329.4 0.8 fusion.75
  330.9 0.8 fusion.75
  333.9 0.8 fusion.75
  423.9 1.6 fusion.16
  425.5 1.2 copy.89
  (610 shorter events, 156.6 us)
Async XLA Ops:
  0.6 5.6 %copy-start = (f32[64,4,8,128]{3,2,1,0:T(8,128)S(1)}, f32[64,4,8,128]{3,2,1,0:T(8,128)}, u32[]{:S(2)}) copy-start(f32[64,4,8,128]{3,2,1,0:T(8,128)} %param.6) | copy-start | bytes 3145732
  3.0 9.8 %collective-permute-start = (f32[64,2,8,128]{3,2,1,0:T(8,128)}, f32[64,2,8,128]{3,2,1,0:T(8,128)S(1)}, u32[]{:S(2)}, u32[]{:S(2)}) collective-permute-start(f32[64,2,8,128]{3,2,1,0:T(8,128)} %get-tuple-element.279), channel_id=1, source_target_pairs={{8,0},{16,8},{24,16},{32,24},{40,32},{48,40},{56,48},{64,56},{72,6... | collective-permute-start | bytes 1572872 | tf_op jit(solution)/shard_map/ppermute | solution.py:18
  6.2 0.7 copy-start.1
  6.2 6.8 %collective-permute-start.1 = (f32[64,2,8,128]{3,2,1,0:T(8,128)}, f32[64,2,8,128]{3,2,1,0:T(8,128)S(1)}, u32[]{:S(2)}, u32[]{:S(2)}) collective-permute-start(f32[64,2,8,128]{3,2,1,0:T(8,128)} %get-tuple-element.278), channel_id=1, source_target_pairs={{0,8},{8,16},{16,24},{24,32},{32,40},{40,48},{48,56},{56,64},{64,7... | collective-permute-start | bytes 1572872 | tf_op jit(solution)/shard_map/ppermute | solution.py:16
  13.6 11.8 %collective-permute-start.2 = (f32[64,8,2,128]{3,1,2,0:T(8,128)S(1)}, f32[64,8,2,128]{3,1,2,0:T(8,128)S(1)}, u32[]{:S(2)}, u32[]{:S(2)}) collective-permute-start(f32[64,8,2,128]{3,1,2,0:T(8,128)S(1)} %get-tuple-element.266), channel_id=1, source_target_pairs={{1,0},{2,1},{3,2},{4,3},{5,4},{6,5},{7,6},{0,7},{9,8},{10,9},{11,1... | collective-permute-start | bytes 1572872 | tf_op jit(solution)/shard_map/ppermute | solution.py:18
  19.3 9.2 %collective-permute-start.3 = (f32[64,8,2,128]{3,1,2,0:T(8,128)S(1)}, f32[64,8,2,128]{3,1,2,0:T(8,128)S(1)}, u32[]{:S(2)}, u32[]{:S(2)}) collective-permute-start(f32[64,8,2,128]{3,1,2,0:T(8,128)S(1)} %get-tuple-element.267), channel_id=1, source_target_pairs={{0,1},{1,2},{2,3},{3,4},{4,5},{5,6},{6,7},{7,0},{8,9},{9,10},{10,1... | collective-permute-start | bytes 1572872 | tf_op jit(solution)/shard_map/ppermute | solution.py:16
  36.4 14.6 %collective-permute-start.4 = (f32[64,2,8,128]{3,2,1,0:T(8,128)S(1)}, f32[64,2,8,128]{3,2,1,0:T(8,128)S(1)}, u32[]{:S(2)}, u32[]{:S(2)}) collective-permute-start(f32[64,2,8,128]{3,2,1,0:T(8,128)S(1)} %copy.74), channel_id=1, source_target_pairs={{8,0},{16,8},{24,16},{32,24},{40,32},{48,40},{56,48},{64,56},{72,6... | collective-permute-start | bytes 1572872 | tf_op jit(solution)/shard_map/ppermute | solution.py:18
  46.1 6.4 %collective-permute-start.5 = (f32[64,2,8,128]{3,2,1,0:T(8,128)S(1)}, f32[64,2,8,128]{3,2,1,0:T(8,128)S(1)}, u32[]{:S(2)}, u32[]{:S(2)}) collective-permute-start(f32[64,2,8,128]{3,2,1,0:T(8,128)S(1)} %copy.76), channel_id=1, source_target_pairs={{0,8},{8,16},{16,24},{24,32},{32,40},{40,48},{48,56},{56,64},{64,7... | collective-permute-start | bytes 1572872 | tf_op jit(solution)/shard_map/ppermute | solution.py:16
  53.2 8.1 %collective-permute-start.6 = (f32[64,8,2,128]{3,1,2,0:T(8,128)S(1)}, f32[64,8,2,128]{3,1,2,0:T(8,128)S(1)}, u32[]{:S(2)}, u32[]{:S(2)}) collective-permute-start(f32[64,8,2,128]{3,1,2,0:T(8,128)S(1)} %get-tuple-element.264), channel_id=1, source_target_pairs={{1,0},{2,1},{3,2},{4,3},{5,4},{6,5},{7,6},{0,7},{9,8},{10,9},{11,1... | collective-permute-start | bytes 1572872 | tf_op jit(solution)/shard_map/ppermute | solution.py:18
  53.3 9.3 %collective-permute-start.7 = (f32[64,8,2,128]{3,1,2,0:T(8,128)S(1)}, f32[64,8,2,128]{3,1,2,0:T(8,128)S(1)}, u32[]{:S(2)}, u32[]{:S(2)}) collective-permute-start(f32[64,8,2,128]{3,1,2,0:T(8,128)S(1)} %get-tuple-element.265), channel_id=1, source_target_pairs={{0,1},{1,2},{2,3},{3,4},{4,5},{5,6},{6,7},{7,0},{8,9},{9,10},{10,1... | collective-permute-start | bytes 1572872 | tf_op jit(solution)/shard_map/ppermute | solution.py:16
  423.9 1.6 copy-start.2
